TPU v7x, 512 devices: a whole 4x4x16 slice. The times are simulated.
512 devices in a mesh: row: 32 (over z, core), col: 16 (over y, x).
Axes of the slice: x: 4, y: 4, z: 16, core: 2. Of those that a mesh axis runs over, the one named last changes fastest.
Arguments:
- tokens: bfloat16 [512, 8192], P('row', 'col'), may hold values from -6 to 6
- out_grad: bfloat16 [512, 8192], P('row', 'col'), may hold values from -1.5 to 1.5
- gate_weight: bfloat16 [8192, 16384], P('col', 'row'), may hold values from -0.0625 to 0.0625
- up_weight: bfloat16 [8192, 16384], P('col', 'row'), may hold values from -0.0625 to 0.0625
- down_weight: bfloat16 [16384, 8192], P('row', 'col'), may hold values from -0.046875 to 0.046875
Outputs:
- input_grad: bfloat16 [512, 8192], P('row', 'col')
- gate_weight_grad: bfloat16 [8192, 16384], P('col', 'row')
- up_weight_grad: bfloat16 [8192, 16384], P('col', 'row')
- down_weight_grad: bfloat16 [16384, 8192], P('row', 'col')
All inputs are finite; a program needn't handle non-finite values.
Results may differ from a plain program's by a relative error of at most 0.005.
Values may be sent and summed in bfloat16 or wider, within the bound.
No kernel may reach another device: no remote copies, remote signals or barrier semaphores. Data moves between devices by JAX's collectives and lax.ppermute only.
A program may use at most 64 MiB of HBM per device.

v0:
```python
import jax
import jax.numpy as jnp
from jax import lax
from jax.sharding import PartitionSpec as P


def pointwise(gate, up, hidden_grad):
    sig = jax.nn.sigmoid(gate)
    act = gate * sig
    hidden = (act * up).astype(jnp.bfloat16)
    gate_grad = (hidden_grad * up * sig * (1.0 + gate * (1.0 - sig))).astype(jnp.bfloat16)
    up_grad = (hidden_grad * act).astype(jnp.bfloat16)
    return (hidden, gate_grad, up_grad)


def body(tokens, out_grad, gate_weight, up_weight, down_weight):
    n_col = lax.psum(1, "col")
    n_row = lax.psum(1, "row")
    rows_all = lax.all_gather(tokens, "row", axis=0, tiled=True)
    grads_all = lax.all_gather(out_grad, "row", axis=0, tiled=True)
    n_tok, width = rows_all.shape
    contract_cols = (((1,), (1,)), ((), ()))
    contract_rows = (((0,), (0,)), ((), ()))
    gate_part = jnp.dot(rows_all, gate_weight, preferred_element_type=jnp.float32)
    up_part = jnp.dot(rows_all, up_weight, preferred_element_type=jnp.float32)
    grad_part = lax.dot_general(
        grads_all, down_weight, contract_cols, preferred_element_type=jnp.float32
    )
    hid = gate_part.shape[1]
    chunk = n_tok // n_col
    parts = jnp.stack([gate_part, up_part, grad_part]).reshape(3, n_col, chunk, hid)
    parts = lax.all_to_all(parts, "col", 1, 1, tiled=True)
    gate, up, hidden_grad = parts.sum(axis=1)
    small = jnp.stack(pointwise(gate, up, hidden_grad))
    spread = jnp.broadcast_to(small[None], (n_col,) + small.shape)
    spread = lax.all_to_all(spread, "col", 0, 0, tiled=True)
    spread = spread.transpose(1, 0, 2, 3).reshape(3, n_tok, hid)
    hidden, gate_grad, up_grad = (spread[0], spread[1], spread[2])
    gate_weight_grad = lax.dot_general(
        rows_all, gate_grad, contract_rows, preferred_element_type=jnp.float32
    ).astype(jnp.bfloat16)
    up_weight_grad = lax.dot_general(
        rows_all, up_grad, contract_rows, preferred_element_type=jnp.float32
    ).astype(jnp.bfloat16)
    down_weight_grad = lax.dot_general(
        hidden, grads_all, contract_rows, preferred_element_type=jnp.float32
    ).astype(jnp.bfloat16)
    total = lax.dot_general(
        gate_grad, gate_weight, contract_cols, preferred_element_type=jnp.float32
    ) + lax.dot_general(up_grad, up_weight, contract_cols, preferred_element_type=jnp.float32)
    total = total.reshape(n_row, n_tok // n_row, width)
    input_grad = lax.all_to_all(total, "row", 0, 0, tiled=True).sum(axis=0)
    return (input_grad.astype(jnp.bfloat16), gate_weight_grad, up_weight_grad, down_weight_grad)


def solution(mesh):
    return jax.shard_map(
        body,
        mesh=mesh,
        in_specs=(
            P("row", "col"),
            P("row", "col"),
            P("col", "row"),
            P("col", "row"),
            P("row", "col"),
        ),
        out_specs=(P("row", "col"), P("col", "row"), P("col", "row"), P("row", "col")),
        check_vma=False,
    )
```

profile of v0, /device:TPU:1, one launch (start us, length us, event | category | flops | bytes accessed | tf_op | source)
XLA Modules:
  0.0 213.3 jit_solution(18360959105764189668)
XLA Ops:
  0.6 0.0 copy-start
  0.6 0.0 copy-start.3
  0.7 39.4 %all_gather.6 = bf16[512,512]{1,0:T(8,128)(2,1)S(1)} all-gather(bf16[16,512]{1,0:T(8,128)(2,1)} %param.5), channel_id=1, replica_groups=mesh['row'=32,'col'=16] {'row'}, dimensions={0}, use_global_device_ids=true | all-gather | bytes 540672 | tf_op jit(solution)/shard_map/all_gather | solution.py:19
  40.0 28.7 %all_gather.7 = bf16[512,512]{1,0:T(8,128)(2,1)S(1)} all-gather(bf16[16,512]{1,0:T(8,128)(2,1)} %param.6), channel_id=1, replica_groups=mesh['row'=32,'col'=16] {'row'}, dimensions={0}, use_global_device_ids=true | all-gather | bytes 540672 | tf_op jit(solution)/shard_map/all_gather | solution.py:20
  68.8 1.5 fusion.5
  70.3 0.0 copy-done
  70.3 0.4 fusion.4
  70.7 0.0 copy-done.3
  70.7 0.5 fusion.6
  71.2 0.5 pad_maximum_fusion
  71.7 45.6 %all_to_all.15 = f32[3,16,32,512]{3,2,0,1:T(8,128)} all-to-all(f32[3,16,32,512]{3,2,0,1:T(8,128)S(1)} %pad_maximum_fusion), channel_id=1, replica_groups=mesh['row'=32,'col'=16] {'col'}, dimensions={1} | all-to-all | bytes 6291456 | tf_op jit(solution)/shard_map/all_to_all | solution.py:32
  117.4 2.2 %reduce_sum.18 = f32[3,32,512]{2,1,0:T(8,128)S(1)} reduce(f32[3,16,32,512]{3,2,0,1:T(8,128)} %all_to_all.15, f32[]{:T(128)} %constant.0.clone.1), dimensions={1}, to_apply=%region_0.0 | reduce | flops 737280 | bytes 3342340 | tf_op jit(solution)/shard_map/reduce_sum | solution.py:33
  119.6 0.2 broadcast_in_dim.2
  119.8 24.6 %all_to_all.16 = bf16[16,3,32,512]{3,2,1,0:T(8,128)(2,1)S(1)} all-to-all(bf16[16,3,32,512]{3,2,1,0:T(8,128)(2,1)S(1)} %broadcast_in_dim.2), channel_id=1, replica_groups=mesh['row'=32,'col'=16] {'col'}, dimensions={0} | all-to-all | bytes 3145728 | tf_op jit(solution)/shard_map/all_to_all | solution.py:36
  144.4 0.0 copy-start.1
  144.4 0.9 fusion.3
  145.3 0.0 copy-start.2
  145.3 0.5 fusion.7
  145.8 0.0 copy-done.1
  145.8 1.4 convolution_add_fusion
  147.3 0.0 copy-done.2
  147.3 9.6 %all-to-all-start.2 = ((f32[32,16,512]{2,1,0:T(8,128)}), f32[32,16,512]{2,1,0:T(8,128)S(1)}, u32[]{:S(2)}, u32[]{:S(2)}) async-start(f32[32,16,512]{2,1,0:T(8,128)} %bitcast.9), calls=%async_computation.2 | async-start | bytes 2097152 | tf_op jit(solution)/shard_map/all_to_all | solution.py:52
  156.9 2.3 %fusion = bf16[512,512]{0,1:T(8,128)(2,1)} fusion(bf16[512,512]{1,0:T(8,128)(2,1)} %bitcast.41, bf16[512,512]{1,0:T(8,128)(2,1)S(1)} %all_gather.6), kind=kOutput, calls=%fused_computation.5 | convolution fusion | flops 268697600 | bytes 1572864 | tf_op jit(solution)/shard_map/dot_general | solution.py:39
  159.2 2.0 copy.14
  161.2 1.3 fusion.1
  162.5 2.0 copy.15
  164.5 2.3 %convolution_convert_fusion = bf16[512,512]{1,0:T(8,128)(2,1)} fusion(bf16[512,512]{1,0:T(8,128)(2,1)} %bitcast.42, bf16[512,512]{1,0:T(8,128)(2,1)S(1)} %all_gather.7), kind=kOutput, calls=%fused_computation.2 | convolution fusion | flops 268697600 | bytes 1572864 | tf_op jit(solution)/shard_map/dot_general | solution.py:45
  166.8 45.8 %all-to-all-done.2 = f32[32,16,512]{2,1,0:T(8,128)S(1)} async-done(((f32[32,16,512]{2,1,0:T(8,128)}), f32[32,16,512]{2,1,0:T(8,128)S(1)}, u32[]{:S(2)}, u32[]{:S(2)}) %all-to-all-start.2) | async-done | bytes 1048608 | tf_op jit(solution)/shard_map/all_to_all | solution.py:52
  212.6 0.7 reduce_sum.19
  (2 shorter events, 0.1 us)
Async XLA Ops:
  0.6 69.6 %copy-start = (bf16[512,512]{1,0:T(8,128)(2,1)S(1)}, bf16[512,512]{1,0:T(8,128)(2,1)}, u32[]{:S(2)}) copy-start(bf16[512,512]{1,0:T(8,128)(2,1)} %param.7) | copy-start | bytes 1572868
  0.6 70.1 %copy-start.3 = (bf16[512,512]{1,0:T(8,128)(2,1)S(1)}, bf16[512,512]{1,0:T(8,128)(2,1)}, u32[]{:S(2)}) copy-start(bf16[512,512]{1,0:T(8,128)(2,1)} %param.9) | copy-start | bytes 1572868
  144.4 1.4 copy-start.1
  145.3 1.9 copy-start.2
  147.3 65.3 %all-to-all-start.2 = ((f32[32,16,512]{2,1,0:T(8,128)}), f32[32,16,512]{2,1,0:T(8,128)S(1)}, u32[]{:S(2)}, u32[]{:S(2)}) async-start(f32[32,16,512]{2,1,0:T(8,128)} %bitcast.9), calls=%async_computation.2 | async-start | bytes 2097152 | tf_op jit(solution)/shard_map/all_to_all | solution.py:52
where the time goes:
time: 214 us; the launch traced here: 213 us
  blocking collectives  138 us (64%)
  waiting for transfers between devices  45.8 us (21%)
  matrix products  10.1 us (5%)
  starting transfers between devices  9.62 us (4%)
  local copies, waits for them, and re-layouts  5.2 us (2%)
  other arithmetic  3.47 us (2%)
    all_to_all x1, waiting for transfers between devices, body(): input_grad = lax.all_to_all(total, 'row', 0, 0, tiled=True).sum(axis=0)  45.8 us
    all_to_all x1, blocking collectives, body(): parts = lax.all_to_all(parts, 'col', 1, 1, tiled=True)  45.6 us
    all_gather x1, blocking collectives, body(): rows_all = lax.all_gather(tokens, 'row', axis=0, tiled=True)  39.4 us
    all_gather x1, blocking collectives, body(): grads_all = lax.all_gather(out_grad, 'row', axis=0, tiled=True)  28.7 us
    all_to_all x1, blocking collectives, body(): spread = lax.all_to_all(spread, 'col', 0, 0, tiled=True)  24.6 us
    all_to_all x1, starting transfers between devices, body(): input_grad = lax.all_to_all(total, 'row', 0, 0, tiled=True).sum(axis=0)  9.62 us
  transfers between devices with their start and end apart: 1, of which 1 were waited for; matrix products, arithmetic and copies ran while one was open for 5% of the time, Pallas kernels for 0%

commit v1 on v0

--- a/solution.py
+++ b/solution.py
@@ -17,7 +17,9 @@
     n_col = lax.psum(1, "col")
     n_row = lax.psum(1, "row")
     rows_all = lax.all_gather(tokens, "row", axis=0, tiled=True)
-    grads_all = lax.all_gather(out_grad, "row", axis=0, tiled=True)
+    grads_all = jnp.concatenate(
+        lax.all_to_all(jnp.stack([out_grad] * lax.axis_size("row")), "row", 0, 0), axis=0
+    )
     n_tok, width = rows_all.shape
     contract_cols = (((1,), (1,)), ((), ()))
     contract_rows = (((0,), (0,)), ((), ()))

time: 214 us -> 220 us (1.028)
  starting transfers between devices: 9.62 us -> 29.4 us
  blocking collectives: 138 us -> 121 us
  waiting for transfers between devices: 45.8 us -> 48.5 us
    all_gather x1 -> x0, blocking collectives: 28.7 us -> none  [body(): grads_all = lax.all_gather(out_grad, 'row', axis=0, tiled=True)]
    all_to_all x0 -> x1, starting transfers between devices: none -> 16.8 us  [body(): lax.all_to_all(jnp.stack([out_grad] * lax.axis_size('row')), 'row', 0, 0)]
    all_gather x1, blocking collectives: 39.4 us -> 51.2 us  [body(): rows_all = lax.all_gather(tokens, 'row', axis=0, tiled=True)]
    all_to_all x1, starting transfers between devices: 9.62 us -> 12.7 us  [body(): input_grad = lax.all_to_all(total, 'row', 0, 0, tiled=True).sum(axis=0)]
    all_to_all x1, waiting for transfers between devices: 45.8 us -> 48.5 us  [body(): input_grad = lax.all_to_all(total, 'row', 0, 0, tiled=True).sum(axis=0)]
  transfers between devices with their start and end apart: 1 -> 2, of which waited for: 1 -> 1; matrix products, arithmetic and copies ran while one was open for 5% -> 4% of each run, Pallas kernels for 0% -> 0%
where the time goes in v1:
time: 220 us; the launch traced here: 219 us
  blocking collectives  121 us (55%)
  waiting for transfers between devices  48.5 us (22%)
  starting transfers between devices  29.4 us (13%)
  matrix products  9.65 us (4%)
  local copies, waits for them, and re-layouts  6.3 us (3%)
  other arithmetic  3.31 us (2%)
    all_gather x1, blocking collectives, body(): rows_all = lax.all_gather(tokens, 'row', axis=0, tiled=True)  51.2 us
    all_to_all x1, waiting for transfers between devices, body(): input_grad = lax.all_to_all(total, 'row', 0, 0, tiled=True).sum(axis=0)  48.5 us
    all_to_all x1, blocking collectives, body(): parts = lax.all_to_all(parts, 'col', 1, 1, tiled=True)  45.6 us
    all_to_all x1, blocking collectives, body(): spread = lax.all_to_all(spread, 'col', 0, 0, tiled=True)  24.6 us
    all_to_all x1, starting transfers between devices, body(): lax.all_to_all(jnp.stack([out_grad] * lax.axis_size('row')), 'row', 0, 0)  16.8 us
    all_to_all x1, starting transfers between devices, body(): input_grad = lax.all_to_all(total, 'row', 0, 0, tiled=True).sum(axis=0)  12.7 us
  transfers between devices with their start and end apart: 2, of which 1 were waited for; matrix products, arithmetic and copies ran while one was open for 4% of the time, Pallas kernels for 0%

profile of v1, /device:TPU:1, one launch (start us, length us, event | category | flops | bytes accessed | tf_op | source)
XLA Modules:
  0.0 219.4 jit_solution(3409906493292522678)
XLA Ops:
  0.6 0.0 copy-start
  0.6 1.6 stack.12
  2.3 16.8 %all-to-all-start = ((bf16[32,16,512]{2,1,0:T(8,128)(2,1)}), bf16[32,16,512]{2,1,0:T(8,128)(2,1)}, u32[]{:S(2)}, u32[]{:S(2)}) async-start(bf16[32,16,512]{2,1,0:T(8,128)(2,1)} %stack.12), calls=%async_computation | async-start | bytes 1048576 | tf_op jit(solution)/shard_map/all_to_all | solution.py:21
  19.1 51.2 %all_gather.3 = bf16[512,512]{1,0:T(8,128)(2,1)S(1)} all-gather(bf16[16,512]{1,0:T(8,128)(2,1)} %param.5), channel_id=1, replica_groups=mesh['row'=32,'col'=16] {'row'}, dimensions={0}, use_global_device_ids=true | all-gather | bytes 540672 | tf_op jit(solution)/shard_map/all_gather | solution.py:19
  70.3 1.5 fusion.6
  71.8 0.0 copy-done
  71.8 0.4 fusion.5
  72.2 0.0 all-to-all-done
  72.2 1.7 convolution_bitcast_fusion
  73.9 0.4 pad_maximum_fusion
  74.3 0.5 copy.11
  74.8 45.6 %all_to_all.20 = f32[3,16,32,512]{3,2,0,1:T(8,128)} all-to-all(f32[3,16,32,512]{3,2,0,1:T(8,128)S(1)} %copy.11), channel_id=1, replica_groups=mesh['row'=32,'col'=16] {'col'}, dimensions={1} | all-to-all | bytes 6291456 | tf_op jit(solution)/shard_map/all_to_all | solution.py:34
  120.5 2.2 %reduce_sum.18 = f32[3,32,512]{2,1,0:T(8,128)S(1)} reduce(f32[3,16,32,512]{3,2,0,1:T(8,128)} %all_to_all.20, f32[]{:T(128)} %constant.0.clone.1), dimensions={1}, to_apply=%region_0.0 | reduce | flops 737280 | bytes 3342340 | tf_op jit(solution)/shard_map/reduce_sum | solution.py:35
  122.7 0.2 broadcast_in_dim.2
  122.9 24.6 %all_to_all.21 = bf16[16,3,32,512]{3,2,1,0:T(8,128)(2,1)S(1)} all-to-all(bf16[16,3,32,512]{3,2,1,0:T(8,128)(2,1)S(1)} %broadcast_in_dim.2), channel_id=1, replica_groups=mesh['row'=32,'col'=16] {'col'}, dimensions={0} | all-to-all | bytes 3145728 | tf_op jit(solution)/shard_map/all_to_all | solution.py:38
  147.5 0.0 copy-start.1
  147.5 0.9 fusion.4
  148.4 0.5 fusion.7
  148.9 0.0 copy-done.1
  148.9 1.4 convolution_add_fusion
  150.3 12.7 %all-to-all-start.3 = ((f32[32,16,512]{2,1,0:T(8,128)}), f32[32,16,512]{2,1,0:T(8,128)S(1)}, u32[]{:S(2)}, u32[]{:S(2)}) async-start(f32[32,16,512]{2,1,0:T(8,128)} %bitcast.8), calls=%async_computation.3 | async-start | bytes 2097152 | tf_op jit(solution)/shard_map/all_to_all | solution.py:54
  163.0 1.3 fusion
  164.2 2.0 copy.12
  166.3 0.5 fusion.1
  166.7 1.0 copy.13
  167.8 2.5 %convolution_convert_fusion = bf16[512,512]{1,0:T(8,128)(2,1)} fusion(bf16[512,512]{1,0:T(8,128)(2,1)} %bitcast.40, bf16[512,512]{1,0:T(8,128)(2,1)} %bitcast.12), kind=kOutput, calls=%fused_computation.3 | convolution fusion | flops 268697600 | bytes 1572864 | tf_op jit(solution)/shard_map/dot_general | solution.py:47
  170.2 48.5 %all-to-all-done.3 = f32[32,16,512]{2,1,0:T(8,128)S(1)} async-done(((f32[32,16,512]{2,1,0:T(8,128)}), f32[32,16,512]{2,1,0:T(8,128)S(1)}, u32[]{:S(2)}, u32[]{:S(2)}) %all-to-all-start.3) | async-done | bytes 1048608 | tf_op jit(solution)/shard_map/all_to_all | solution.py:54
  218.7 0.7 reduce_sum.19
  (2 shorter events, 0.1 us)
Async XLA Ops:
  0.6 71.1 %copy-start = (bf16[512,512]{1,0:T(8,128)(2,1)S(1)}, bf16[512,512]{1,0:T(8,128)(2,1)}, u32[]{:S(2)}) copy-start(bf16[512,512]{1,0:T(8,128)(2,1)} %param.7) | copy-start | bytes 1572868
  2.3 69.9 %all-to-all-start = ((bf16[32,16,512]{2,1,0:T(8,128)(2,1)}), bf16[32,16,512]{2,1,0:T(8,128)(2,1)}, u32[]{:S(2)}, u32[]{:S(2)}) async-start(bf16[32,16,512]{2,1,0:T(8,128)(2,1)} %stack.12), calls=%async_computation | async-start | bytes 1048576 | tf_op jit(solution)/shard_map/all_to_all | solution.py:21
  147.5 1.4 copy-start.1
  150.3 68.4 %all-to-all-start.3 = ((f32[32,16,512]{2,1,0:T(8,128)}), f32[32,16,512]{2,1,0:T(8,128)S(1)}, u32[]{:S(2)}, u32[]{:S(2)}) async-start(f32[32,16,512]{2,1,0:T(8,128)} %bitcast.8), calls=%async_computation.3 | async-start | bytes 2097152 | tf_op jit(solution)/shard_map/all_to_all | solution.py:54
